TPU v7x, 32 devices: a whole 2x2x4 slice. The times are simulated.
32 devices in a mesh: slab: 8 (over y, x, core), view: 4 (over z).
Axes of the slice: x: 2, y: 2, z: 4, core: 2. Of those that a mesh axis runs over, the one named last changes fastest.
Arguments:
- estimate: float32 [4, 1024, 1024], P(None, 'slab'), may hold values from 0.5 to 2
- views: float32 [4, 4, 1024, 1024], P('view', None, 'slab'), may hold values from 0.25 to 4
- psf: float32 [4, 1024, 1024], P('view', 'slab'), as said below
- pattern_mult: int32 [4, 8], P('view'), may hold values from 0 to 63
- pattern_shift: int32 [4, 8], P('view'), may hold values from 0 to 127
- interp: float32 [4, 8, 128], P('view'), may hold values from 0.05 to 0.45
Outputs:
- updated: float32 [4, 1024, 1024], P(None, 'slab')
Inputs may be any that keep to these rules, and one draw needn't show every extreme that they name: `psf`: every entry is positive.
All inputs are finite; a program needn't handle non-finite values.
Results may differ from a plain program's by a relative error of at most 0.0001.
Values sent between devices are 32-bit elements; how exact they have to be, the bound alone decides.
No kernel may reach another device: no remote copies, remote signals or barrier semaphores. Data moves between devices by JAX's collectives and lax.ppermute only.
A program may use at most 128 MiB of HBM per device.

v0:
```python
import math
import jax
import jax.numpy as jnp
from jax import lax
from jax.sharding import PartitionSpec as P

highest = lax.Precision.HIGHEST


def block_matrix(multiplier, shifting, weights):
    positions = jnp.arange(128, dtype=jnp.int32)
    first_col = ((2 * multiplier[:, None] + 1) * positions[None, :] + shifting[:, None]) % 128
    second_col = (first_col + 1) % 128
    columns = positions[None, None, :]
    lower = (columns == first_col[:, :, None]).astype(jnp.float32)
    upper = (columns == second_col[:, :, None]).astype(jnp.float32)
    return (1.0 - weights)[:, :, None] * lower + weights[:, :, None] * upper


def angle_tables(rows, cols, length):
    row_index = lax.iota(jnp.int32, rows)[:, None]
    col_index = lax.iota(jnp.int32, cols)[None, :]
    angles = (row_index * col_index % length).astype(jnp.float32) * (2.0 * math.pi / length)
    return (jnp.cos(angles), jnp.sin(angles))


def contract(form, real_part, imag_part, cosine, sine_table, direction, want_imag):
    real_cos = jnp.einsum(form, real_part, cosine, precision=highest)
    if imag_part is None:
        return (real_cos, direction * jnp.einsum(form, real_part, sine_table, precision=highest))
    imag_sin = jnp.einsum(form, imag_part, sine_table, precision=highest)
    out_real = real_cos - direction * imag_sin
    if not want_imag:
        return (out_real, None)
    real_sin = jnp.einsum(form, real_part, sine_table, precision=highest)
    imag_cos = jnp.einsum(form, imag_part, cosine, precision=highest)
    return (out_real, imag_cos + direction * real_sin)


def complex_times(real_part, imag_part, cosine, sine_table):
    return (
        real_part * cosine - imag_part * sine_table,
        real_part * sine_table + imag_part * cosine,
    )


def factored(real_part, imag_part, axis, direction, forward, want_imag):
    length = real_part.shape[axis]
    second = 128
    first = length // second
    if axis == 2:
        leading, trailing = ("rx", "")
    else:
        leading, trailing = ("r", "z")
    outer = real_part.shape
    shape = outer[:axis] + (first, second) + outer[axis + 1 :]
    real_part = real_part.reshape(shape)
    if imag_part is not None:
        imag_part = imag_part.reshape(shape)
    first_cos, first_sin = angle_tables(first, first, first)
    second_cos, second_sin = angle_tables(second, second, second)
    twist_cos, twist_sin = angle_tables(first, second, length)
    if axis == 1:
        twist_cos = twist_cos[:, :, None]
        twist_sin = twist_sin[:, :, None]
    twist_sin = direction * twist_sin
    if forward:
        real_part, imag_part = contract(
            leading + "ab" + trailing + ",ak->" + leading + "kb" + trailing,
            real_part,
            imag_part,
            first_cos,
            first_sin,
            direction,
            True,
        )
        real_part, imag_part = complex_times(real_part, imag_part, twist_cos, twist_sin)
        real_part, imag_part = contract(
            leading + "kb" + trailing + ",bm->" + leading + "km" + trailing,
            real_part,
            imag_part,
            second_cos,
            second_sin,
            direction,
            want_imag,
        )
    else:
        real_part, imag_part = contract(
            leading + "km" + trailing + ",mb->" + leading + "kb" + trailing,
            real_part,
            imag_part,
            second_cos,
            second_sin,
            direction,
            True,
        )
        real_part, imag_part = complex_times(real_part, imag_part, twist_cos, twist_sin)
        real_part, imag_part = contract(
            leading + "kb" + trailing + ",ka->" + leading + "ab" + trailing,
            real_part,
            imag_part,
            first_cos,
            first_sin,
            direction,
            want_imag,
        )
    real_part = real_part.reshape(outer)
    if imag_part is not None:
        imag_part = imag_part.reshape(outer)
    return (real_part, imag_part)


def to_columns(real_part, imag_part):
    depth_real, depth_imag = factored(real_part, imag_part, 2, -1.0, True, True)
    moved_real, moved_imag = (
        lax.all_to_all(depth_real, "slab", split_axis=2, concat_axis=1, tiled=True),
        lax.all_to_all(depth_imag, "slab", split_axis=2, concat_axis=1, tiled=True),
    )
    return factored(moved_real, moved_imag, 1, -1.0, True, True)


def to_planes(real_part, imag_part):
    width_real, width_imag = factored(real_part, imag_part, 1, 1.0, False, True)
    moved_real, moved_imag = (
        lax.all_to_all(width_real, "slab", split_axis=1, concat_axis=2, tiled=True),
        lax.all_to_all(width_imag, "slab", split_axis=1, concat_axis=2, tiled=True),
    )
    scaling = 1.0 / (width_real.shape[1] * moved_real.shape[2])
    out_real, out_imag = factored(moved_real, moved_imag, 2, 1.0, False, False)
    return (out_real * scaling, None)


def shards(estimate, views, psf, pattern_mult, pattern_shift, interp):
    row_count, slab_width, depth = estimate.shape
    blocks = block_matrix(pattern_mult[0], pattern_shift[0], interp[0])
    block_count = depth // 128
    shaped = estimate.reshape(row_count, slab_width, block_count, 128)
    sampled = jnp.einsum("bij,yxbj->yxbi", blocks, shaped, precision=highest).reshape(
        row_count, slab_width, depth
    )

    def pack(volume):
        return (volume, None)

    packed_real, packed_imag = pack(sampled)
    packed_real = jnp.concatenate([packed_real, psf], 0)
    spectra_real, spectra_imag = to_columns(packed_real, packed_imag)
    transfer_real = spectra_real[-1:]
    transfer_imag = spectra_imag[-1:]
    spectra_real = spectra_real[:-1]
    spectra_imag = spectra_imag[:-1]
    filtered_real = spectra_real * transfer_real - spectra_imag * transfer_imag
    filtered_imag = spectra_real * transfer_imag + spectra_imag * transfer_real
    blurred_real, blurred_imag = to_planes(filtered_real, filtered_imag)
    quotient = views[0] / blurred_real
    packed_real, packed_imag = pack(quotient)
    spectra_real, spectra_imag = to_columns(packed_real, packed_imag)
    filtered_real = spectra_real * transfer_real + spectra_imag * transfer_imag
    filtered_imag = spectra_imag * transfer_real - spectra_real * transfer_imag
    smeared_real, smeared_imag = to_planes(filtered_real, filtered_imag)
    correction = jnp.einsum(
        "bij,yxbi->yxbj",
        blocks,
        smeared_real.reshape(row_count, slab_width, block_count, 128),
        precision=highest,
    ).reshape(row_count, slab_width, depth)
    log_terms = jnp.log(correction)
    view_count = lax.axis_size("view")
    summed = lax.psum(log_terms, "view")
    return estimate * jnp.exp(summed / view_count)


def solution(mesh):
    placed = (
        P(None, "slab", None),
        P("view", None, "slab", None),
        P("view", "slab", None),
        P("view", None),
        P("view", None),
        P("view", None, None),
    )
    return jax.shard_map(
        shards, mesh=mesh, in_specs=placed, out_specs=P(None, "slab", None), check_vma=False
    )
```

profile of v0, /device:TPU:0, one launch (start us, length us, event | category | flops | bytes accessed | tf_op | source)
XLA Modules:
  0.0 555.8 jit_solution(18437681724977504398)
XLA Ops:
  20.8 4.7 subtract_bitcast_fusion.2
  35.7 5.2 all-to-all-start.1
  50.7 39.3 %all-to-all-done.1 = f32[5,128,1024]{1,0,2:T(8,128)} async-done(((f32[5,128,1024]{1,0,2:T(8,128)}), f32[5,128,1024]{1,0,2:T(8,128)}, u32[]{:S(2)}, u32[]{:S(2)}) %all-to-all-start.1) | async-done | bytes 2621472 | tf_op jit(solution)/shard_map/all_to_all | solution.py:117
  90.0 4.8 all-to-all-start
  98.1 3.8 fusion
  101.9 3.9 fusion.2
  105.8 37.9 %all-to-all-done = f32[5,128,1024]{1,0,2:T(8,128)} async-done(((f32[5,128,1024]{1,0,2:T(8,128)}), f32[5,128,1024]{1,0,2:T(8,128)}, u32[]{:S(2)}, u32[]{:S(2)}) %all-to-all-start) | async-done | bytes 2621472 | tf_op jit(solution)/shard_map/all_to_all | solution.py:116
  146.8 4.3 multiply_add_fusion
  185.9 4.4 all-to-all-start.2
  190.3 4.5 fusion.75
  200.9 16.1 %all-to-all-done.2 = f32[4,1024,128]{2,0,1:T(4,128)} async-done(((f32[4,1024,128]{2,0,1:T(4,128)}), f32[4,1024,128]{2,0,1:T(4,128)}, u32[]{:S(2)}, u32[]{:S(2)}) %all-to-all-start.2) | async-done | bytes 2097184 | tf_op jit(solution)/shard_map/all_to_all | solution.py:125
  217.0 4.5 all-to-all-start.3
  228.4 19.5 %all-to-all-done.3 = f32[4,1024,128]{2,0,1:T(4,128)} async-done(((f32[4,1024,128]{2,0,1:T(4,128)}), f32[4,1024,128]{2,0,1:T(4,128)}, u32[]{:S(2)}, u32[]{:S(2)}) %all-to-all-start.3) | async-done | bytes 2097184 | tf_op jit(solution)/shard_map/all_to_all | solution.py:126
  275.3 4.4 all-to-all-start.5
  279.6 4.0 fusion.69
  289.0 17.3 %all-to-all-done.5 = f32[4,128,1024]{1,0,2:T(4,128)} async-done(((f32[4,128,1024]{1,0,2:T(4,128)}), f32[4,128,1024]{1,0,2:T(4,128)}, u32[]{:S(2)}, u32[]{:S(2)}) %all-to-all-start.5) | async-done | bytes 2097184 | tf_op jit(solution)/shard_map/all_to_all | solution.py:117
  306.3 4.5 all-to-all-start.4
  319.5 17.8 %all-to-all-done.4 = f32[4,128,1024]{1,0,2:T(4,128)} async-done(((f32[4,128,1024]{1,0,2:T(4,128)}), f32[4,128,1024]{1,0,2:T(4,128)}, u32[]{:S(2)}, u32[]{:S(2)}) %all-to-all-start.4) | async-done | bytes 2097184 | tf_op jit(solution)/shard_map/all_to_all | solution.py:116
  375.3 4.4 all-to-all-start.6
  379.6 4.5 fusion.51
  390.2 16.1 %all-to-all-done.6 = f32[4,1024,128]{2,0,1:T(4,128)} async-done(((f32[4,1024,128]{2,0,1:T(4,128)}), f32[4,1024,128]{2,0,1:T(4,128)}, u32[]{:S(2)}, u32[]{:S(2)}) %all-to-all-start.6) | async-done | bytes 2097184 | tf_op jit(solution)/shard_map/all_to_all | solution.py:125
  406.3 4.3 all-to-all-start.7
  416.0 21.3 %all-to-all-done.7 = f32[4,1024,128]{2,0,1:T(4,128)} async-done(((f32[4,1024,128]{2,0,1:T(4,128)}), f32[4,1024,128]{2,0,1:T(4,128)}, u32[]{:S(2)}, u32[]{:S(2)}) %all-to-all-start.7) | async-done | bytes 2097184 | tf_op jit(solution)/shard_map/all_to_all | solution.py:126
  457.7 84.9 %all-reduce.2.cloned.1.call-done = f32[4,128,1024]{1,2,0:T(8,128)} async-done(((f32[4,128,1024]{1,2,0:T(8,128)}), f32[4,128,1024]{1,2,0:T(8,128)}) %all-reduce.2.cloned.1.call-update) | async-done | bytes 2097168 | tf_op jit(solution)/shard_map/psum | solution.py:169
  (116 shorter events, 205.1 us)
Async XLA Ops:
  18.4 2.4 copy-start
  25.5 3.1 copy-start.1
  35.7 54.4 %all-to-all-start.1 = ((f32[5,128,1024]{1,0,2:T(8,128)}), f32[5,128,1024]{1,0,2:T(8,128)}, u32[]{:S(2)}, u32[]{:S(2)}) async-start(f32[5,128,1024]{1,0,2:T(8,128)} %copy.157), calls=%async_computation.1 | async-start | bytes 8388608 | tf_op jit(solution)/shard_map/all_to_all | solution.py:117
  40.8 3.0 copy-start.2
  90.0 53.7 %all-to-all-start = ((f32[5,128,1024]{1,0,2:T(8,128)}), f32[5,128,1024]{1,0,2:T(8,128)}, u32[]{:S(2)}, u32[]{:S(2)}) async-start(f32[5,128,1024]{1,0,2:T(8,128)} %copy.151), calls=%async_computation | async-start | bytes 8388608 | tf_op jit(solution)/shard_map/all_to_all | solution.py:116
  146.8 4.3 copy-start.6
  176.7 3.3 copy-start.4
  185.9 31.0 %all-to-all-start.2 = ((f32[4,1024,128]{2,0,1:T(4,128)}), f32[4,1024,128]{2,0,1:T(4,128)}, u32[]{:S(2)}, u32[]{:S(2)}) async-start(f32[4,1024,128]{2,0,1:T(4,128)} %copy.176), calls=%async_computation.2 | async-start | bytes 4194304 | tf_op jit(solution)/shard_map/all_to_all | solution.py:125
  200.9 20.6 %copy-start.10 = (f32[1,4,128,1024]{3,2,1,0:T(8,128)S(1)}, f32[1,4,128,1024]{3,2,1,0:T(8,128)}, u32[]{:S(2)}) copy-start(f32[1,4,128,1024]{3,2,1,0:T(8,128)} %param.7) | copy-start | bytes 6291460
  217.0 31.0 %all-to-all-start.3 = ((f32[4,1024,128]{2,0,1:T(4,128)}), f32[4,1024,128]{2,0,1:T(4,128)}, u32[]{:S(2)}, u32[]{:S(2)}) async-start(f32[4,1024,128]{2,0,1:T(4,128)} %copy.181), calls=%async_computation.3 | async-start | bytes 4194304 | tf_op jit(solution)/shard_map/all_to_all | solution.py:126
  249.7 2.1 copy-start.7
  256.5 3.1 copy-start.11
  267.1 2.5 copy-start.5
  275.3 31.0 %all-to-all-start.5 = ((f32[4,128,1024]{1,0,2:T(4,128)}), f32[4,128,1024]{1,0,2:T(4,128)}, u32[]{:S(2)}, u32[]{:S(2)}) async-start(f32[4,128,1024]{1,0,2:T(4,128)} %copy.195), calls=%async_computation.5 | async-start | bytes 4194304 | tf_op jit(solution)/shard_map/all_to_all | solution.py:117
  306.3 31.0 %all-to-all-start.4 = ((f32[4,128,1024]{1,0,2:T(4,128)}), f32[4,128,1024]{1,0,2:T(4,128)}, u32[]{:S(2)}, u32[]{:S(2)}) async-start(f32[4,128,1024]{1,0,2:T(4,128)} %copy.189), calls=%async_computation.4 | async-start | bytes 4194304 | tf_op jit(solution)/shard_map/all_to_all | solution.py:116
  339.6 3.7 copy-start.9
  366.2 2.9 copy-start.3
  375.3 31.0 %all-to-all-start.6 = ((f32[4,1024,128]{2,0,1:T(4,128)}), f32[4,1024,128]{2,0,1:T(4,128)}, u32[]{:S(2)}, u32[]{:S(2)}) async-start(f32[4,1024,128]{2,0,1:T(4,128)} %copy.214), calls=%async_computation.6 | async-start | bytes 4194304 | tf_op jit(solution)/shard_map/all_to_all | solution.py:125
  406.3 31.0 %all-to-all-start.7 = ((f32[4,1024,128]{2,0,1:T(4,128)}), f32[4,1024,128]{2,0,1:T(4,128)}, u32[]{:S(2)}, u32[]{:S(2)}) async-start(f32[4,1024,128]{2,0,1:T(4,128)} %copy.219), calls=%async_computation.7 | async-start | bytes 4194304 | tf_op jit(solution)/shard_map/all_to_all | solution.py:126
  410.6 132.0 %all-reduce.2.cloned.1.call-start = ((), (), s32[]{:S(2)}) async-start(), calls=%async_computation.8 | async-start | bytes 4194304 | tf_op jit(solution)/shard_map/psum | solution.py:169
  439.0 2.1 copy-start.8
  448.7 3.3 copy-start.12
Sparse Core Ops, SparseCore 0:
  455.9 86.6 all-reduce.1
where the time goes:
time: 560 us; the launch traced here: 556 us
  waiting for transfers between devices  270 us (48%)
  matrix products  172 us (31%)
  local copies, waits for them, and re-layouts  55.7 us (10%)
  starting transfers between devices  36.6 us (7%)
  between operations  14.4 us (3%)
  other arithmetic  7.07 us (1%)
    psum x1, waiting for transfers between devices, shards(): summed = lax.psum(log_terms, 'view')  84.9 us
    all_to_all x2, waiting for transfers between devices, to_columns(): lax.all_to_all(depth_imag, 'slab', split_axis=2, concat_axis=1, tiled=True)  56.6 us
    all_to_all x2, waiting for transfers between devices, to_columns(): lax.all_to_all(depth_real, 'slab', split_axis=2, concat_axis=1, tiled=True)  55.7 us
    dot_general x16, matrix products, contract(): real_cos = jnp.einsum(form, real_part, cosine, precision=highest)  48.2 us
    dot_general x14, matrix products, contract(): imag_sin = jnp.einsum(form, imag_part, sine_table, precision=highest)  41.1 us
    all_to_all x2, waiting for transfers between devices, to_planes(): lax.all_to_all(width_imag, 'slab', split_axis=1, concat_axis=2, tiled=True)  40.8 us
    dot_general x12, matrix products, contract(): real_sin = jnp.einsum(form, real_part, sine_table, precision=highest)  36.4 us
    dot_general x12, matrix products, contract(): imag_cos = jnp.einsum(form, imag_part, cosine, precision=highest)  35.7 us
  transfers between devices with their start and end apart: 9, of which 9 were waited for; matrix products, arithmetic and copies ran while one was open for 13% of the time, Pallas kernels for 0%

commit v1 on v0

--- a/solution.py
+++ b/solution.py
@@ -122,7 +122,12 @@
 def to_planes(real_part, imag_part):
     width_real, width_imag = factored(real_part, imag_part, 1, 1.0, False, True)
     moved_real, moved_imag = (
-        lax.all_to_all(width_real, "slab", split_axis=1, concat_axis=2, tiled=True),
+        jnp.concatenate(
+            lax.all_to_all(
+                jnp.stack(jnp.split(width_real, lax.axis_size("slab"), axis=1)), "slab", 0, 0
+            ),
+            axis=2,
+        ),
         lax.all_to_all(width_imag, "slab", split_axis=1, concat_axis=2, tiled=True),
     )
     scaling = 1.0 / (width_real.shape[1] * moved_real.shape[2])

time: 560 us -> 566 us (1.011)
    unnamed x29 -> x37, local copies, waits for them, and re-layouts: 5.07 us -> 16.6 us
    reshape x4 -> x2, local copies, waits for them, and re-layouts: 11.8 us -> 6.32 us  [factored(): real_part = real_part.reshape(outer)]
where the time goes in v1:
time: 566 us; the launch traced here: 562 us
  waiting for transfers between devices  271 us (48%)
  matrix products  174 us (31%)
  local copies, waits for them, and re-layouts  59.6 us (11%)
  starting transfers between devices  35.1 us (6%)
  between operations  14.4 us (3%)
  other arithmetic  7.08 us (1%)
    psum x1, waiting for transfers between devices, shards(): summed = lax.psum(log_terms, 'view')  84.9 us
    all_to_all x2, waiting for transfers between devices, to_columns(): lax.all_to_all(depth_imag, 'slab', split_axis=2, concat_axis=1, tiled=True)  56.6 us
    all_to_all x2, waiting for transfers between devices, to_columns(): lax.all_to_all(depth_real, 'slab', split_axis=2, concat_axis=1, tiled=True)  55.7 us
    dot_general x16, matrix products, contract(): real_cos = jnp.einsum(form, real_part, cosine, precision=highest)  49.4 us
    dot_general x14, matrix products, contract(): imag_sin = jnp.einsum(form, imag_part, sine_table, precision=highest)  43.5 us
    all_to_all x2, waiting for transfers between devices, to_planes(): lax.all_to_all(width_imag, 'slab', split_axis=1, concat_axis=2, tiled=True)  41.8 us
    dot_general x12, matrix products, contract(): real_sin = jnp.einsum(form, real_part, sine_table, precision=highest)  36.3 us
    dot_general x12, matrix products, contract(): imag_cos = jnp.einsum(form, imag_part, cosine, precision=highest)  35.1 us
  transfers between devices with their start and end apart: 9, of which 9 were waited for; matrix products, arithmetic and copies ran while one was open for 13% of the time, Pallas kernels for 0%

profile of v1, /device:TPU:0, one launch (start us, length us, event | category | flops | bytes accessed | tf_op | source)
XLA Modules:
  0.0 562.1 jit_solution(16927393408936299826)
XLA Ops:
  20.8 4.7 subtract_bitcast_fusion.2
  31.9 3.8 copy.171
  35.7 5.2 all-to-all-start.1
  50.7 39.3 %all-to-all-done.1 = f32[5,128,1024]{1,0,2:T(8,128)} async-done(((f32[5,128,1024]{1,0,2:T(8,128)}), f32[5,128,1024]{1,0,2:T(8,128)}, u32[]{:S(2)}, u32[]{:S(2)}) %all-to-all-start.1) | async-done | bytes 2621472 | tf_op jit(solution)/shard_map/all_to_all | solution.py:117
  90.1 4.8 all-to-all-start
  98.1 3.8 fusion
  102.0 3.9 fusion.2
  105.8 37.9 %all-to-all-done = f32[5,128,1024]{1,0,2:T(8,128)} async-done(((f32[5,128,1024]{1,0,2:T(8,128)}), f32[5,128,1024]{1,0,2:T(8,128)}, u32[]{:S(2)}, u32[]{:S(2)}) %all-to-all-start) | async-done | bytes 2621472 | tf_op jit(solution)/shard_map/all_to_all | solution.py:116
  146.8 4.3 multiply_add_fusion
  192.1 4.3 all-to-all-start.3
  202.2 20.9 %all-to-all-done.3 = f32[4,1024,128]{2,0,1:T(4,128)} async-done(((f32[4,1024,128]{2,0,1:T(4,128)}), f32[4,1024,128]{2,0,1:T(4,128)}, u32[]{:S(2)}, u32[]{:S(2)}) %all-to-all-start.3) | async-done | bytes 2097184 | tf_op jit(solution)/shard_map/all_to_all | solution.py:131
  223.1 3.8 all-to-all-start.2
  238.8 14.5 %all-to-all-done.2 = f32[8,4,128,128]{3,2,1,0:T(8,128)S(1)} async-done(((f32[8,4,128,128]{3,2,1,0:T(8,128)}), f32[8,4,128,128]{3,2,1,0:T(8,128)S(1)}, u32[]{:S(2)}, u32[]{:S(2)}) %all-to-all-start.2) | async-done | bytes 2097184 | tf_op jit(solution)/shard_map/all_to_all | solution.py:126
  253.3 3.9 fusion.133
  278.5 4.4 all-to-all-start.5
  282.9 4.0 fusion.79
  292.3 17.3 %all-to-all-done.5 = f32[4,128,1024]{1,0,2:T(4,128)} async-done(((f32[4,128,1024]{1,0,2:T(4,128)}), f32[4,128,1024]{1,0,2:T(4,128)}, u32[]{:S(2)}, u32[]{:S(2)}) %all-to-all-start.5) | async-done | bytes 2097184 | tf_op jit(solution)/shard_map/all_to_all | solution.py:117
  309.5 4.5 all-to-all-start.4
  322.7 17.8 %all-to-all-done.4 = f32[4,128,1024]{1,0,2:T(4,128)} async-done(((f32[4,128,1024]{1,0,2:T(4,128)}), f32[4,128,1024]{1,0,2:T(4,128)}, u32[]{:S(2)}, u32[]{:S(2)}) %all-to-all-start.4) | async-done | bytes 2097184 | tf_op jit(solution)/shard_map/all_to_all | solution.py:116
  384.5 4.3 all-to-all-start.7
  394.6 20.9 %all-to-all-done.7 = f32[4,1024,128]{2,0,1:T(4,128)} async-done(((f32[4,1024,128]{2,0,1:T(4,128)}), f32[4,1024,128]{2,0,1:T(4,128)}, u32[]{:S(2)}, u32[]{:S(2)}) %all-to-all-start.7) | async-done | bytes 2097184 | tf_op jit(solution)/shard_map/all_to_all | solution.py:131
  427.9 17.8 %all-to-all-done.6 = f32[8,4,128,128]{3,2,1,0:T(8,128)S(1)} async-done(((f32[8,4,128,128]{3,2,1,0:T(8,128)}), f32[8,4,128,128]{3,2,1,0:T(8,128)S(1)}, u32[]{:S(2)}, u32[]{:S(2)}) %all-to-all-start.6) | async-done | bytes 2097184 | tf_op jit(solution)/shard_map/all_to_all | solution.py:126
  445.7 3.9 fusion.139
  464.0 84.9 %all-reduce.2.cloned.1.call-done = f32[4,128,1024]{1,2,0:T(8,128)} async-done(((f32[4,128,1024]{1,2,0:T(8,128)}), f32[4,128,1024]{1,2,0:T(8,128)}) %all-reduce.2.cloned.1.call-update) | async-done | bytes 2097168 | tf_op jit(solution)/shard_map/psum | solution.py:174
  (122 shorter events, 212.7 us)
Async XLA Ops:
  18.4 2.4 copy-start
  25.5 3.1 copy-start.1
  35.7 54.4 %all-to-all-start.1 = ((f32[5,128,1024]{1,0,2:T(8,128)}), f32[5,128,1024]{1,0,2:T(8,128)}, u32[]{:S(2)}, u32[]{:S(2)}) async-start(f32[5,128,1024]{1,0,2:T(8,128)} %copy.171), calls=%async_computation.1 | async-start | bytes 8388608 | tf_op jit(solution)/shard_map/all_to_all | solution.py:117
  40.8 3.1 copy-start.2
  90.1 53.7 %all-to-all-start = ((f32[5,128,1024]{1,0,2:T(8,128)}), f32[5,128,1024]{1,0,2:T(8,128)}, u32[]{:S(2)}, u32[]{:S(2)}) async-start(f32[5,128,1024]{1,0,2:T(8,128)} %copy.165), calls=%async_computation | async-start | bytes 8388608 | tf_op jit(solution)/shard_map/all_to_all | solution.py:116
  146.8 4.3 copy-start.4
  192.1 31.0 %all-to-all-start.3 = ((f32[4,1024,128]{2,0,1:T(4,128)}), f32[4,1024,128]{2,0,1:T(4,128)}, u32[]{:S(2)}, u32[]{:S(2)}) async-start(f32[4,1024,128]{2,0,1:T(4,128)} %copy.194), calls=%async_computation.3 | async-start | bytes 4194304 | tf_op jit(solution)/shard_map/all_to_all | solution.py:131
  223.1 30.2 %all-to-all-start.2 = ((f32[8,4,128,128]{3,2,1,0:T(8,128)}), f32[8,4,128,128]{3,2,1,0:T(8,128)S(1)}, u32[]{:S(2)}, u32[]{:S(2)}) async-start(f32[8,4,128,128]{3,2,1,0:T(8,128)} %fusion.158), calls=%async_computation.2 | async-start | bytes 4194304 | tf_op jit(solution)/shard_map/all_to_all | solution.py:126
  253.3 3.9 copy-start.7
  259.7 3.1 copy-start.8
  270.4 2.5 copy-start.3
  278.5 31.0 %all-to-all-start.5 = ((f32[4,128,1024]{1,0,2:T(4,128)}), f32[4,128,1024]{1,0,2:T(4,128)}, u32[]{:S(2)}, u32[]{:S(2)}) async-start(f32[4,128,1024]{1,0,2:T(4,128)} %copy.208), calls=%async_computation.5 | async-start | bytes 4194304 | tf_op jit(solution)/shard_map/all_to_all | solution.py:117
  309.5 31.0 %all-to-all-start.4 = ((f32[4,128,1024]{1,0,2:T(4,128)}), f32[4,128,1024]{1,0,2:T(4,128)}, u32[]{:S(2)}, u32[]{:S(2)}) async-start(f32[4,128,1024]{1,0,2:T(4,128)} %copy.202), calls=%async_computation.4 | async-start | bytes 4194304 | tf_op jit(solution)/shard_map/all_to_all | solution.py:116
  342.8 3.7 copy-start.5
  384.5 31.0 %all-to-all-start.7 = ((f32[4,1024,128]{2,0,1:T(4,128)}), f32[4,1024,128]{2,0,1:T(4,128)}, u32[]{:S(2)}, u32[]{:S(2)}) async-start(f32[4,1024,128]{2,0,1:T(4,128)} %copy.231), calls=%async_computation.7 | async-start | bytes 4194304 | tf_op jit(solution)/shard_map/all_to_all | solution.py:131
  415.5 30.2 %all-to-all-start.6 = ((f32[8,4,128,128]{3,2,1,0:T(8,128)}), f32[8,4,128,128]{3,2,1,0:T(8,128)S(1)}, u32[]{:S(2)}, u32[]{:S(2)}) async-start(f32[8,4,128,128]{3,2,1,0:T(8,128)} %fusion.150), calls=%async_computation.6 | async-start | bytes 4194304 | tf_op jit(solution)/shard_map/all_to_all | solution.py:126
  419.1 129.8 %all-reduce.2.cloned.1.call-start = ((), (), s32[]{:S(2)}) async-start(), calls=%async_computation.8 | async-start | bytes 4194304 | tf_op jit(solution)/shard_map/psum | solution.py:174
  445.7 3.9 copy-start.6
  455.0 3.3 copy-start.9
Sparse Core Ops, SparseCore 0:
  462.2 86.6 all-reduce.1
